TPU v7x, 32 devices: a whole 2x2x4 slice. The times are simulated.
32 devices in a mesh: parts: 2 (over y), tm: 4 (over x, core), cols: 4 (over z).
Axes of the slice: x: 2, y: 2, z: 4, core: 2. Of those that a mesh axis runs over, the one named last changes fastest.
Arguments:
- noise: float32 [16, 1024, 1024], P(('parts', 'tm'), None, 'cols'), parts along dimension 0, may hold values from -6 to 6
- inv_diag: float32 [16, 1024, 1024], P(('parts', 'tm'), None, 'cols'), parts along dimension 0, may hold values from -2 to 2, as said below
- coupling: float32 [16, 1024, 1024], P(('parts', 'tm'), None, 'cols'), parts along dimension 0, may hold values from -1 to 1, as said below
- order: int32 [1024], replicated, may hold values from 0 to 1023, each once
Outputs:
- sample: float32 [16, 1024, 1024], P(('parts', 'tm'), None, 'cols'), parts along dimension 0
There are 2 independent parts, one for each index of `parts`. A program takes and returns all parts, laid end to end along the dimension named above; an argument that names none is the same for every part. Nothing has to cross between parts.
Inputs may be any that keep to these rules, and one draw needn't show every extreme that they name: `order`: each of 0 to 1023 appears once. `inv_diag`: diagonal entries lie between 0.5 and 2, off-diagonal entries are small in magnitude. `coupling`: diagonal entries lie between 0.5 and 0.97, off-diagonal entries are small in magnitude.
All inputs are finite; a program needn't handle non-finite values.
Results may differ from a plain program's by a relative error of at most 0.00013.
Values sent between devices are 32-bit elements; how exact they have to be, the bound alone decides.
No kernel may reach another device: no remote copies, remote signals or barrier semaphores. Data moves between devices by JAX's collectives and lax.ppermute only.
A program may use at most 128 MiB of HBM per device.

v0:
```python
import jax
import jax.numpy as jnp
from jax import lax
from jax.sharding import PartitionSpec as P

low = jnp.bfloat16


def shifted(block, axis, distance):
    devices = range(lax.axis_size(axis))
    route = [(i - distance, i) for i in devices if i - distance in devices]
    return lax.ppermute(block, axis, route)


def split(value, count):
    parts = []
    rest = value
    for index in range(count):
        kept = lax.reduce_precision(rest, exponent_bits=8, mantissa_bits=7)
        parts.append(kept.astype(low))
        if index < count - 1:
            rest = rest - kept
    return parts


def bdot(left, right):
    return jnp.dot(left, right, preferred_element_type=jnp.float32)


def apply(matrix_parts, operand):
    high, small = matrix_parts
    operand_high, operand_small = split(operand, 2)
    return bdot(high, operand_high) + (bdot(high, operand_small) + bdot(small, operand_high))


def shards(noise, inv_diag, coupling, order):
    block_count = noise.shape[0]
    node_count = noise.shape[1]
    sample_count = noise.shape[2]
    pieces = 2 if sample_count % 256 == 0 else 1
    width = sample_count // pieces
    inv_full = lax.all_gather(inv_diag, "cols", axis=2, tiled=True)
    coupling_parts = [
        split(lax.all_gather(coupling[block], "cols", axis=1, tiled=True), 2)
        for block in range(block_count)
    ]
    driven = [apply(split(inv_full[block], 2), noise[block]) for block in range(block_count)]
    driven_pieces = [
        [driven[block][:, p * width : (p + 1) * width] for p in range(pieces)]
        for block in range(block_count)
    ]

    def chain(entering, piece, skip_last):
        carried = entering
        results = [None] * block_count
        for block in range(block_count - 1, -1, -1):
            if skip_last and block == block_count - 1:
                carried = driven_pieces[block][piece]
            else:
                carried = driven_pieces[block][piece] + apply(coupling_parts[block], carried)
            results[block] = carried
        return results

    first = [shifted(chain(None, p, True)[0], "tm", -1) for p in range(pieces)]

    def relay_step(step, entering):
        return [shifted(chain(entering[p], p, False)[0], "tm", -1) for p in range(pieces)]

    entering = lax.fori_loop(0, lax.axis_size("tm") - 2, relay_step, first)
    finals = [chain(entering[p], p, False) for p in range(pieces)]
    selector = (order[:, None] == jnp.arange(node_count, dtype=order.dtype)[None, :]).astype(low)
    outputs = []
    for block in range(block_count):
        field = jnp.concatenate([finals[p][block] for p in range(pieces)], axis=1)
        top, middle, bottom = split(field, 3)
        outputs.append(bdot(selector, top) + (bdot(selector, middle) + bdot(selector, bottom)))
    return jnp.stack(outputs, axis=0)


def solution(mesh):
    return jax.shard_map(
        shards,
        mesh=mesh,
        in_specs=(
            P(("parts", "tm"), None, "cols"),
            P(("parts", "tm"), None, "cols"),
            P(("parts", "tm"), None, "cols"),
            P(),
        ),
        out_specs=P(("parts", "tm"), None, "cols"),
        check_vma=False,
    )
```

profile of v0, /device:TPU:1, one launch (start us, length us, event | category | flops | bytes accessed | tf_op | source)
XLA Modules:
  0.0 439.5 jit_solution(6839977181822519246)
XLA Ops:
  6.5 3.0 fusion.150
  11.0 81.5 %all-gather.8.cloned.1.call-done = f32[1,1024,1024]{2,1,0:T(8,128)} async-done(((f32[1,1024,256]{2,1,0:T(8,128)}), f32[1,1024,1024]{2,1,0:T(8,128)}) %all-gather.8.cloned.1.call-update) | async-done | bytes 4194320 | tf_op jit(solution)/shard_map/all_gather | solution.py:44
  92.6 4.4 %reduce-precision_convert_fusion.13 = (bf16[1024,1024]{1,0:T(8,128)(2,1)S(1)}, bf16[1024,1024]{1,0:T(8,128)(2,1)}) fusion(f32[1,1024,1024]{2,1,0:T(8,128)} %all-gather.8.cloned.1.call-done), kind=kLoop, calls=%fused_computation.43 | loop fusion | flops 5242880 | bytes 8388608 | tf_op jit(solution)/shard_map/convert_element_type | solution.py:20
  97.0 76.5 %all-gather.10.cloned.1.call-done = f32[1,1024,1024]{2,1,0:T(8,128)} async-done(((f32[1,1024,256]{2,1,0:T(8,128)}), f32[1,1024,1024]{2,1,0:T(8,128)}) %all-gather.10.cloned.1.call-update) | async-done | bytes 4194320 | tf_op jit(solution)/shard_map/all_gather | solution.py:44
  173.5 5.0 %reduce-precision_convert_fusion.12 = (bf16[1024,1024]{1,0:T(8,128)(2,1)}, bf16[1024,1024]{1,0:T(8,128)(2,1)}) fusion(f32[1,1024,1024]{2,1,0:T(8,128)} %all-gather.10.cloned.1.call-done), kind=kLoop, calls=%fused_computation.41 | loop fusion | flops 5242880 | bytes 8388608 | tf_op jit(solution)/shard_map/convert_element_type | solution.py:20
  178.5 144.9 %all-gather.6.cloned.1.call-done = f32[2,1024,1024]{2,1,0:T(8,128)} async-done(((f32[2,1024,256]{2,1,0:T(8,128)}), f32[2,1024,1024]{2,1,0:T(8,128)}) %all-gather.6.cloned.1.call-update) | async-done | bytes 8388624 | tf_op jit(solution)/shard_map/all_gather | solution.py:42
  323.4 3.4 fusion.47
  326.9 3.8 fusion.97
  341.5 2.4 collective-permute-start.2
  343.8 2.1 collective-permute-start.3
  347.0 2.0 copy.10
  349.0 2.0 copy.9
  351.1 2.3 fusion.151
  353.4 4.4 %collective-permute-done.3 = f32[1024,128]{0,1:T(8,128)S(1)} collective-permute-done((f32[1024,128]{0,1:T(8,128)}, f32[1024,128]{0,1:T(8,128)S(1)}, u32[]{:S(2)}, u32[]{:S(2)}) %collective-permute-start.3) | collective-permute-done | bytes 524320 | tf_op jit(solution)/shard_map/ppermute | solution.py:12
  357.8 54.2 %while.12 = (s32[]{:T(128)}, f32[1024,128]{0,1:T(8,128)S(1)}, f32[1024,128]{0,1:T(8,128)S(1)}, bf16[1024,1024]{1,0:T(8,128)(2,1)}, bf16[1024,1024]{1,0:T(8,128)(...) while((s32[]{:T(128)}, f32[1024,128]{0,1:T(8,128)S(1)}, ...), condition=%wide.region_1.0_spmd, body=%wide.region_0.0_spmd.sunk | while | flops 3226992640 | bytes 81789320 | solution.py:69
  357.8 2.5 fusion.228
  366.2 1.9 collective-permute-start
  374.2 1.9 collective-permute-start.1
  376.9 8.0 %collective-permute-done.1 = f32[1024,128]{0,1:T(8,128)S(1)} collective-permute-done((f32[1024,128]{0,1:T(8,128)}, f32[1024,128]{0,1:T(8,128)S(1)}, u32[]{:S(2)}, u32[]{:S(2)}) %collective-permute-start.1) | collective-permute-done | bytes 524320 | tf_op jit(solution)/shard_map/while/body/eval_jaxpr/ppermute | solution.py:12
  384.9 2.5 fusion.228
  393.3 1.9 collective-permute-start
  401.3 1.9 collective-permute-start.1
  404.0 8.0 %collective-permute-done.1 = f32[1024,128]{0,1:T(8,128)S(1)} collective-permute-done((f32[1024,128]{0,1:T(8,128)}, f32[1024,128]{0,1:T(8,128)S(1)}, u32[]{:S(2)}, u32[]{:S(2)}) %collective-permute-start.1) | collective-permute-done | bytes 524320 | tf_op jit(solution)/shard_map/while/body/eval_jaxpr/ppermute | solution.py:12
  412.0 2.6 fusion.136
  (110 shorter events, 56.8 us)
Async XLA Ops:
  6.5 86.0 %all-gather.8.cloned.1.call-start = ((), (), s32[]{:S(2)}) async-start(), calls=%async_computation.1 | async-start | bytes 5242880 | tf_op jit(solution)/shard_map/all_gather | solution.py:44
  9.6 163.9 %all-gather.10.cloned.1.call-start = ((), (), s32[]{:S(2)}) async-start(), calls=%async_computation.2 | async-start | bytes 5242880 | tf_op jit(solution)/shard_map/all_gather | solution.py:44
  10.3 313.1 %all-gather.6.cloned.1.call-start = ((), (), s32[]{:S(2)}) async-start(), calls=%async_computation | async-start | bytes 10485760 | tf_op jit(solution)/shard_map/all_gather | solution.py:42
  323.4 7.2 %copy-start.7 = (f32[2,1024,1024]{2,1,0:T(8,128)S(1)}, f32[2,1024,1024]{2,1,0:T(8,128)}, u32[]{:S(2)}) copy-start(f32[2,1024,1024]{2,1,0:T(8,128)} %all-gather.6.cloned.1.call-done) | copy-start | bytes 25165828
  326.8 4.0 copy-start.14
  331.6 14.3 %copy-start.8 = (f32[1024,256]{0,1:T(8,128)}, f32[1024,256]{0,1:T(8,128)S(1)}, u32[]{:S(2)}) copy-start(f32[1024,256]{0,1:T(8,128)S(1)} %fusion.69) | copy-start | bytes 3145732
  338.1 1.7 copy-start.15
  341.5 11.9 %collective-permute-start.2 = (f32[1024,128]{0,1:T(8,128)}, f32[1024,128]{0,1:T(8,128)S(1)}, u32[]{:S(2)}, u32[]{:S(2)}) collective-permute-start(f32[1024,128]{0,1:T(8,128)} %fusion.71), channel_id=1, source_target_pairs={{4,0},{8,4},{12,8},{5,1},{9,5},{13,9},{6,2},{10,6},{14,10},{7,3},{... | collective-permute-start | bytes 1572872 | tf_op jit(solution)/shard_map/ppermute | solution.py:12
  343.8 14.0 %collective-permute-start.3 = (f32[1024,128]{0,1:T(8,128)}, f32[1024,128]{0,1:T(8,128)S(1)}, u32[]{:S(2)}, u32[]{:S(2)}) collective-permute-start(f32[1024,128]{0,1:T(8,128)} %fusion.74), channel_id=1, source_target_pairs={{4,0},{8,4},{12,8},{5,1},{9,5},{13,9},{6,2},{10,6},{14,10},{7,3},{... | collective-permute-start | bytes 1572872 | tf_op jit(solution)/shard_map/ppermute | solution.py:12
  357.8 2.5 copy-start
  362.9 1.6 copy-start.3
  362.9 1.7 copy-start.13
  364.5 3.6 copy-start.5
  366.2 10.7 %collective-permute-start = (f32[1024,128]{0,1:T(8,128)}, f32[1024,128]{0,1:T(8,128)S(1)}, u32[]{:S(2)}, u32[]{:S(2)}) collective-permute-start(f32[1024,128]{0,1:T(8,128)} %fusion.232), channel_id=1, source_target_pairs={{4,0},{8,4},{12,8},{5,1},{9,5},{13,9},{6,2},{10,6},{14,10},{7,3},{... | collective-permute-start | bytes 1572872 | tf_op jit(solution)/shard_map/while/body/eval_jaxpr/ppermute | solution.py:12
  374.2 10.7 %collective-permute-start.1 = (f32[1024,128]{0,1:T(8,128)}, f32[1024,128]{0,1:T(8,128)S(1)}, u32[]{:S(2)}, u32[]{:S(2)}) collective-permute-start(f32[1024,128]{0,1:T(8,128)} %fusion.238), channel_id=1, source_target_pairs={{4,0},{8,4},{12,8},{5,1},{9,5},{13,9},{6,2},{10,6},{14,10},{7,3},{... | collective-permute-start | bytes 1572872 | tf_op jit(solution)/shard_map/while/body/eval_jaxpr/ppermute | solution.py:12
  384.9 2.5 copy-start
  390.0 1.6 copy-start.3
  390.0 1.7 copy-start.13
  391.6 3.6 copy-start.5
  393.3 10.7 %collective-permute-start = (f32[1024,128]{0,1:T(8,128)}, f32[1024,128]{0,1:T(8,128)S(1)}, u32[]{:S(2)}, u32[]{:S(2)}) collective-permute-start(f32[1024,128]{0,1:T(8,128)} %fusion.232), channel_id=1, source_target_pairs={{4,0},{8,4},{12,8},{5,1},{9,5},{13,9},{6,2},{10,6},{14,10},{7,3},{... | collective-permute-start | bytes 1572872 | tf_op jit(solution)/shard_map/while/body/eval_jaxpr/ppermute | solution.py:12
  401.3 10.7 %collective-permute-start.1 = (f32[1024,128]{0,1:T(8,128)}, f32[1024,128]{0,1:T(8,128)S(1)}, u32[]{:S(2)}, u32[]{:S(2)}) collective-permute-start(f32[1024,128]{0,1:T(8,128)} %fusion.238), channel_id=1, source_target_pairs={{4,0},{8,4},{12,8},{5,1},{9,5},{13,9},{6,2},{10,6},{14,10},{7,3},{... | collective-permute-start | bytes 1572872 | tf_op jit(solution)/shard_map/while/body/eval_jaxpr/ppermute | solution.py:12
  412.0 2.6 copy-start.6
  414.6 1.6 copy-start.1
  419.1 1.6 copy-start.4
  (10 other events, 11.2 us)
Sparse Core Ops, SparseCore 0:
  9.7 82.8 all-gather.7
  94.1 79.2 all-gather.9
  175.0 148.3 all-gather.5
where the time goes:
time: 440 us; the launch traced here: 439 us
  waiting for transfers between devices  326 us (74%)
  matrix products  59.5 us (14%)
  local copies, waits for them, and re-layouts  16.8 us (4%)
  between operations  13.4 us (3%)
  starting transfers between devices  12.2 us (3%)
  other arithmetic  10.9 us (2%)
    all_gather x2, waiting for transfers between devices, shards(): lax.all_gather(coupling[block], 'cols', axis=1, tiled=True)  158 us
    all_gather x1, waiting for transfers between devices, shards(): inv_full = lax.all_gather(inv_diag, 'cols', axis=2, tiled=True)  145 us
    dot_general x54, matrix products, bdot(): return jnp.dot(left, right, preferred_element_type=jnp.float32)  59.5 us
    ppermute x6, waiting for transfers between devices, shifted(): return lax.ppermute(block, axis, route)  22 us
    ppermute x6, starting transfers between devices, shifted(): return lax.ppermute(block, axis, route)  12.1 us
    convert_element_type x2, other arithmetic, split(): parts.append(kept.astype(low))  9.48 us
  transfers between devices with their start and end apart: 9, of which 8 were waited for; matrix products, arithmetic and copies ran while one was open for 6% of the time, Pallas kernels for 0%

commit v1 on v0

--- a/solution.py
+++ b/solution.py
@@ -39,7 +39,12 @@
     sample_count = noise.shape[2]
     pieces = 2 if sample_count % 256 == 0 else 1
     width = sample_count // pieces
-    inv_full = lax.all_gather(inv_diag, "cols", axis=2, tiled=True)
+    ring = [inv_diag]
+    for hop in range(3):
+        ring.append(lax.ppermute(ring[-1], "cols", [(dev, (dev + 1) % 4) for dev in range(4)]))
+    inv_full = jnp.roll(
+        jnp.concatenate(ring[::-1], axis=2), (lax.axis_index("cols") + 1) * ring[0].shape[2], axis=2
+    )
     coupling_parts = [
         split(lax.all_gather(coupling[block], "cols", axis=1, tiled=True), 2)
         for block in range(block_count)

time: 440 us -> 413 us (0.939)
  the two profiles are of different devices: /device:TPU:1 before, /device:TPU:17 now
where the time goes in v1:
time: 413 us; the launch traced here: 412 us
  waiting for transfers between devices  277 us (67%)
  matrix products  54.9 us (13%)
  starting transfers between devices  28.3 us (7%)
  local copies, waits for them, and re-layouts  28.2 us (7%)
  between operations  13.9 us (3%)
  other arithmetic  9.94 us (2%)
    ppermute x3, waiting for transfers between devices, shards(): lax.ppermute(ring[-1], 'cols', [(dev, (dev + 1) % 4) for dev in range(4)])  259 us
    dot_general x54, matrix products, bdot(): return jnp.dot(left, right, preferred_element_type=jnp.float32)  54.9 us
    ppermute x6, starting transfers between devices, shifted(): return lax.ppermute(block, axis, route)  24.6 us
    ppermute x6, waiting for transfers between devices, shifted(): return lax.ppermute(block, axis, route)  17.6 us
    unnamed x37, local copies, waits for them, and re-layouts  14 us
    convert_element_type x2, other arithmetic, split(): parts.append(kept.astype(low))  8.48 us
  transfers between devices with their start and end apart: 11, of which 7 were waited for; matrix products, arithmetic and copies ran while one was open for 11% of the time, Pallas kernels for 0%

profile of v1, /device:TPU:17, one launch (start us, length us, event | category | flops | bytes accessed | tf_op | source)
XLA Modules:
  0.0 412.2 jit_solution(7142200775461406472)
XLA Ops:
  6.5 3.1 fusion.150
  11.1 112.7 %collective-permute-done.2 = f32[2,1024,256]{2,1,0:T(8,128)S(1)} collective-permute-done((f32[2,1024,256]{2,1,0:T(8,128)S(1)}, f32[2,1024,256]{2,1,0:T(8,128)S(1)}, u32[]{:S(2)}, u32[]{:S(2)}) %collective-permute-start.2) | collective-permute-done | bytes 2097184 | tf_op jit(solution)/shard_map/ppermute | solution.py:44
  126.3 44.6 %collective-permute-done.3 = f32[2,1024,256]{2,1,0:T(8,128)} collective-permute-done((f32[2,1024,256]{2,1,0:T(8,128)S(1)}, f32[2,1024,256]{2,1,0:T(8,128)}, u32[]{:S(2)}, u32[]{:S(2)}) %collective-permute-start.3) | collective-permute-done | bytes 2097184 | tf_op jit(solution)/shard_map/ppermute | solution.py:44
  172.1 101.8 %collective-permute-done.4 = f32[2,1024,256]{2,1,0:T(8,128)} collective-permute-done((f32[2,1024,256]{2,1,0:T(8,128)}, f32[2,1024,256]{2,1,0:T(8,128)}, u32[]{:S(2)}, u32[]{:S(2)}) %collective-permute-start.4) | collective-permute-done | bytes 2097184 | tf_op jit(solution)/shard_map/ppermute | solution.py:44
  273.8 1.9 constant_dynamic-update-slice_fusion.7
  275.7 2.1 constant_dynamic-update-slice_fusion.6
  278.5 1.9 constant_dynamic-update-slice_fusion.3
  280.5 1.9 constant_dynamic-update-slice_fusion.2
  290.2 3.3 reduce-precision_convert_fusion.13
  297.2 14.9 %collective-permute-start.6 = (f32[1024,128]{0,1:T(8,128)}, f32[1024,128]{0,1:T(8,128)S(1)}, u32[]{:S(2)}, u32[]{:S(2)}) collective-permute-start(f32[1024,128]{0,1:T(8,128)} %fusion.70), channel_id=1, source_target_pairs={{4,0},{8,4},{12,8},{5,1},{9,5},{13,9},{6,2},{10,6},{14,10},{7,3},{... | collective-permute-start | bytes 1572872 | tf_op jit(solution)/shard_map/ppermute | solution.py:12
  316.5 2.1 collective-permute-start.5
  319.6 2.1 copy.10
  321.7 2.0 copy.9
  323.8 5.2 %reduce-precision_convert_fusion.12 = (bf16[1024,1024]{1,0:T(8,128)(2,1)}, bf16[1024,1024]{1,0:T(8,128)(2,1)}) fusion(f32[1,1024,1024]{2,1,0:T(8,128)} %all-gather.7.cloned.1.call-done), kind=kLoop, calls=%fused_computation.41 | loop fusion | flops 5242880 | bytes 8388608 | tf_op jit(solution)/shard_map/convert_element_type | solution.py:20
  329.0 55.5 %while.12 = (s32[]{:T(128)}, f32[1024,128]{0,1:T(8,128)S(1)}, f32[1024,128]{0,1:T(8,128)S(1)}, bf16[1024,1024]{1,0:T(8,128)(2,1)}, bf16[1024,1024]{1,0:T(8,128)(...) while((s32[]{:T(128)}, f32[1024,128]{0,1:T(8,128)S(1)}, ...), condition=%wide.region_1.2_spmd, body=%wide.region_0.1_spmd.sunk | while | flops 3226992640 | bytes 81789320 | solution.py:74
  329.0 2.5 fusion.233
  338.0 1.9 collective-permute-start.1
  346.0 1.9 collective-permute-start
  348.7 8.0 %collective-permute-done = f32[1024,128]{0,1:T(8,128)S(1)} collective-permute-done((f32[1024,128]{0,1:T(8,128)}, f32[1024,128]{0,1:T(8,128)S(1)}, u32[]{:S(2)}, u32[]{:S(2)}) %collective-permute-start) | collective-permute-done | bytes 524320 | tf_op jit(solution)/shard_map/while/body/eval_jaxpr/ppermute | solution.py:12
  356.7 2.4 fusion.233
  365.8 1.9 collective-permute-start.1
  373.8 1.9 collective-permute-start
  376.5 8.0 %collective-permute-done = f32[1024,128]{0,1:T(8,128)S(1)} collective-permute-done((f32[1024,128]{0,1:T(8,128)}, f32[1024,128]{0,1:T(8,128)S(1)}, u32[]{:S(2)}, u32[]{:S(2)}) %collective-permute-start) | collective-permute-done | bytes 524320 | tf_op jit(solution)/shard_map/while/body/eval_jaxpr/ppermute | solution.py:12
  384.5 2.6 fusion.128
  (129 shorter events, 67.4 us)
Async XLA Ops:
  6.5 3.2 copy-start.18
  6.5 283.6 %all-gather.5.cloned.1.call-start = ((), (), s32[]{:S(2)}) async-start(), calls=%async_computation | async-start | bytes 5242880 | tf_op jit(solution)/shard_map/all_gather | solution.py:49
  9.7 314.1 %all-gather.7.cloned.1.call-start = ((), (), s32[]{:S(2)}) async-start(), calls=%async_computation.1 | async-start | bytes 5242880 | tf_op jit(solution)/shard_map/all_gather | solution.py:49
  9.7 114.1 %collective-permute-start.2 = (f32[2,1024,256]{2,1,0:T(8,128)S(1)}, f32[2,1024,256]{2,1,0:T(8,128)S(1)}, u32[]{:S(2)}, u32[]{:S(2)}) collective-permute-start(f32[2,1024,256]{2,1,0:T(8,128)S(1)} %copy-done.18), channel_id=1, source_target_pairs={{0,1},{1,2},{2,3},{3,0},{4,5},{5,6},{6,7},{7,4},{8,9},{9,10},{10,1... | collective-permute-start | bytes 6291464 | tf_op jit(solution)/shard_map/ppermute | solution.py:44
  125.1 45.8 %collective-permute-start.3 = (f32[2,1024,256]{2,1,0:T(8,128)S(1)}, f32[2,1024,256]{2,1,0:T(8,128)}, u32[]{:S(2)}, u32[]{:S(2)}) collective-permute-start(f32[2,1024,256]{2,1,0:T(8,128)S(1)} %collective-permute-done.2), channel_id=1, source_target_pairs={{0,1},{1,2},{2,3},{3,0},{4,5},{5,6},{6,7},{7,4},{8,9},{9,10},{10,1... | collective-permute-start | bytes 6291464 | tf_op jit(solution)/shard_map/ppermute | solution.py:44
  170.9 102.9 %collective-permute-start.4 = (f32[2,1024,256]{2,1,0:T(8,128)}, f32[2,1024,256]{2,1,0:T(8,128)}, u32[]{:S(2)}, u32[]{:S(2)}) collective-permute-start(f32[2,1024,256]{2,1,0:T(8,128)} %collective-permute-done.3), channel_id=1, source_target_pairs={{0,1},{1,2},{2,3},{3,0},{4,5},{5,6},{6,7},{7,4},{8,9},{9,10},{10,1... | collective-permute-start | bytes 6291464 | tf_op jit(solution)/shard_map/ppermute | solution.py:44
  275.7 2.2 copy-start.20
  286.6 2.0 copy-start.15
  290.1 5.0 %copy-start.7 = (f32[1024,256]{0,1:T(8,128)}, f32[1024,256]{0,1:T(8,128)S(1)}, u32[]{:S(2)}) copy-start(f32[1024,256]{0,1:T(8,128)S(1)} %convolution_add_fusion.3) | copy-start | bytes 3145732
  293.5 18.7 %copy-start.2 = (bf16[1024,1024]{1,0:T(8,128)(2,1)}, bf16[1024,1024]{1,0:T(8,128)(2,1)S(1)}, u32[]{:S(2)}) copy-start(bf16[1024,1024]{1,0:T(8,128)(2,1)S(1)} %get-tuple-element.182) | copy-start | bytes 6291460
  297.2 16.8 %copy-start.8 = (f32[1024,256]{0,1:T(8,128)S(1)}, f32[1024,256]{0,1:T(8,128)}, u32[]{:S(2)}) copy-start(f32[1024,256]{0,1:T(8,128)} %copy-done.7) | copy-start | bytes 3145732
  297.2 31.8 %collective-permute-start.6 = (f32[1024,128]{0,1:T(8,128)}, f32[1024,128]{0,1:T(8,128)S(1)}, u32[]{:S(2)}, u32[]{:S(2)}) collective-permute-start(f32[1024,128]{0,1:T(8,128)} %fusion.70), channel_id=1, source_target_pairs={{4,0},{8,4},{12,8},{5,1},{9,5},{13,9},{6,2},{10,6},{14,10},{7,3},{... | collective-permute-start | bytes 1572872 | tf_op jit(solution)/shard_map/ppermute | solution.py:12
  316.5 12.5 %collective-permute-start.5 = (f32[1024,128]{0,1:T(8,128)}, f32[1024,128]{0,1:T(8,128)S(1)}, u32[]{:S(2)}, u32[]{:S(2)}) collective-permute-start(f32[1024,128]{0,1:T(8,128)} %fusion.67), channel_id=1, source_target_pairs={{4,0},{8,4},{12,8},{5,1},{9,5},{13,9},{6,2},{10,6},{14,10},{7,3},{... | collective-permute-start | bytes 1572872 | tf_op jit(solution)/shard_map/ppermute | solution.py:12
  329.0 2.5 copy-start.5
  331.5 1.7 copy-start.10
  334.7 1.7 copy-start.12
  338.0 10.7 %collective-permute-start.1 = (f32[1024,128]{0,1:T(8,128)}, f32[1024,128]{0,1:T(8,128)S(1)}, u32[]{:S(2)}, u32[]{:S(2)}) collective-permute-start(f32[1024,128]{0,1:T(8,128)} %fusion.238), channel_id=1, source_target_pairs={{4,0},{8,4},{12,8},{5,1},{9,5},{13,9},{6,2},{10,6},{14,10},{7,3},{... | collective-permute-start | bytes 1572872 | tf_op jit(solution)/shard_map/while/body/eval_jaxpr/ppermute | solution.py:12
  346.0 10.7 %collective-permute-start = (f32[1024,128]{0,1:T(8,128)}, f32[1024,128]{0,1:T(8,128)S(1)}, u32[]{:S(2)}, u32[]{:S(2)}) collective-permute-start(f32[1024,128]{0,1:T(8,128)} %fusion.232), channel_id=1, source_target_pairs={{4,0},{8,4},{12,8},{5,1},{9,5},{13,9},{6,2},{10,6},{14,10},{7,3},{... | collective-permute-start | bytes 1572872 | tf_op jit(solution)/shard_map/while/body/eval_jaxpr/ppermute | solution.py:12
  356.7 2.5 copy-start.5
  359.2 1.7 copy-start.10
  362.4 1.7 copy-start.12
  365.8 10.7 %collective-permute-start.1 = (f32[1024,128]{0,1:T(8,128)}, f32[1024,128]{0,1:T(8,128)S(1)}, u32[]{:S(2)}, u32[]{:S(2)}) collective-permute-start(f32[1024,128]{0,1:T(8,128)} %fusion.238), channel_id=1, source_target_pairs={{4,0},{8,4},{12,8},{5,1},{9,5},{13,9},{6,2},{10,6},{14,10},{7,3},{... | collective-permute-start | bytes 1572872 | tf_op jit(solution)/shard_map/while/body/eval_jaxpr/ppermute | solution.py:12
  373.8 10.7 %collective-permute-start = (f32[1024,128]{0,1:T(8,128)}, f32[1024,128]{0,1:T(8,128)S(1)}, u32[]{:S(2)}, u32[]{:S(2)}) collective-permute-start(f32[1024,128]{0,1:T(8,128)} %fusion.232), channel_id=1, source_target_pairs={{4,0},{8,4},{12,8},{5,1},{9,5},{13,9},{6,2},{10,6},{14,10},{7,3},{... | collective-permute-start | bytes 1572872 | tf_op jit(solution)/shard_map/while/body/eval_jaxpr/ppermute | solution.py:12
  384.5 2.6 copy-start.1
  (16 other events, 21.2 us)
Sparse Core Ops, SparseCore 0:
  9.8 115.4 all-gather.4
  172.2 116.3 all-gather.6
